TPU v7x, 256 devices: a whole 4x4x8 slice. The times are simulated.
256 devices in a mesh: dp: 8 (over x, core), seq: 32 (over y, z).
Axes of the slice: x: 4, y: 4, z: 8, core: 2. Of those that a mesh axis runs over, the one named last changes fastest.
Arguments:
- activations: bfloat16 [8, 4096, 2048], P('dp', 'seq'), may hold values from -16 to 16
- w_query: bfloat16 [2048, 2048], P('seq')
- w_key: bfloat16 [2048, 256], P('seq')
- w_value: bfloat16 [2048, 256], P('seq'), may hold values from -0.125 to 0.125
- key_blocks: int32 [32, 32, 7], replicated, may hold values from 0 to 31, as said below
- random_count: int32 [32], replicated, may hold values from 1 to 3, 64 in all
- grad_out: bfloat16 [8, 4096, 2048], P('dp', 'seq'), may hold values from -6 to 6
Outputs:
- attn_out: bfloat16 [8, 4096, 2048], P('dp', 'seq')
- grad_x: bfloat16 [8, 4096, 2048], P('dp', 'seq')
- grad_wq: bfloat16 [2048, 2048], P('seq')
- grad_wk: bfloat16 [2048, 256], P('seq')
- grad_wv: bfloat16 [2048, 256], P('seq')
Inputs may be any that keep to these rules, and one draw needn't show every extreme that they name: `key_blocks`: row b of head h: columns 0 to 2 are b - 1, b and b + 1 modulo 32; column 3 is one block of the head, the same in all its rows; columns 4 to 6 are three blocks that differ from each other and from the row's first four entries. Head h uses the first random_count[h] of its three random key blocks; the counts sum to 64.
All inputs are finite; a program needn't handle non-finite values.
Results may differ from a plain program's by a relative error of at most 0.025.
The roundings to bfloat16 on the way count: a program that leaves them out, or rounds other values in their place, can miss the bound.
Values may be sent and summed in bfloat16 or wider, within the bound.
No kernel may reach another device: no remote copies, remote signals or barrier semaphores. Data moves between devices by JAX's collectives and lax.ppermute only.
A program may use at most 128 MiB of HBM per device.

v0:
```python
import math
import jax
import jax.numpy as jnp
from jax import lax
from jax.sharding import PartitionSpec as P

HD = 64
GROUP = 8
masked_score = -1e30
query_group = 4
RING_Z = 8


def head_pass(queries, key_rows, value_rows, grad_head, blocks, extra_count):
    seq_len, head_width = queries.shape
    block_count, slot_count = blocks.shape
    block_len = seq_len // block_count
    score_scale = head_width ** (-0.5)
    key_tiles = key_rows.reshape(block_count, block_len, head_width)
    value_tiles = value_rows.reshape(block_count, block_len, head_width)
    q_part = queries.reshape(block_count, block_len, head_width)
    g_part = grad_head.reshape(block_count, block_len, head_width)
    usable = jnp.repeat(jnp.arange(slot_count) < 4 + extra_count, block_len)
    k_part = key_tiles[blocks].reshape(block_count, slot_count * block_len, head_width)
    v_part = value_tiles[blocks].reshape(block_count, slot_count * block_len, head_width)
    scores = (
        jnp.einsum("gqe,gke->gqk", q_part, k_part, preferred_element_type=jnp.float32) * score_scale
    )
    scores = jnp.where(usable, scores, masked_score)
    highest = jnp.max(scores, axis=-1, keepdims=True)
    exponent = jnp.exp(scores - highest)
    shares = exponent / jnp.sum(exponent, axis=-1, keepdims=True)
    shares_low = shares.astype(jnp.bfloat16)
    attended = jnp.einsum(
        "gqk,gke->gqe", shares_low, v_part, preferred_element_type=jnp.float32
    ).astype(jnp.bfloat16)
    grad_shares = jnp.einsum("gqe,gke->gqk", g_part, v_part, preferred_element_type=jnp.float32)
    weighted = jnp.sum(grad_shares * shares, axis=-1, keepdims=True)
    grad_scores = (shares * (grad_shares - weighted)).astype(jnp.bfloat16)
    grad_query = (
        jnp.einsum("gqk,gke->gqe", grad_scores, k_part, preferred_element_type=jnp.float32)
        * score_scale
    ).astype(jnp.bfloat16)
    grad_keys = (
        jnp.einsum("gqk,gqe->gke", grad_scores, q_part, preferred_element_type=jnp.float32)
        * score_scale
    )
    grad_values = jnp.einsum("gqk,gqe->gke", shares_low, g_part, preferred_element_type=jnp.float32)
    pieces = jnp.concatenate([grad_keys, grad_values], axis=-1).reshape(
        block_count * slot_count, block_len * 2 * head_width
    )
    owner = (
        blocks.reshape(1, block_count * slot_count)
        == jnp.arange(block_count, dtype=blocks.dtype)[:, None]
    ).astype(jnp.float32)
    summed = jnp.dot(owner, pieces, precision=lax.Precision.HIGHEST)
    return (
        attended.reshape(seq_len, head_width),
        grad_query.reshape(seq_len, head_width),
        summed.reshape(seq_len, 2 * head_width),
    )


def ring_reduce_scatter(parts, ring, stride, position):
    seq_devices = lax.axis_size("seq")
    group = ring * stride
    me = position // stride % ring
    width = parts.shape[-1] // 2
    ahead = [
        (s, s // group * group + (s // stride % ring + 1) % ring * stride + s % stride)
        for s in range(seq_devices)
    ]
    behind = [(b, a) for a, b in ahead]
    total = []
    for side, perm, sign in ((0, ahead, 1), (1, behind, -1)):
        own = parts[..., side * width : (side + 1) * width]

        def chunk(k):
            return lax.dynamic_index_in_dim(own, (me - sign * (1 + k)) % ring, 0, keepdims=False)

        buf = chunk(0)
        for k in range(ring - 1):
            got = lax.ppermute(buf, "seq", perm)
            buf = (got.astype(jnp.float32) + chunk(k + 1).astype(jnp.float32)).astype(jnp.bfloat16)
        total.append(buf)
    return jnp.concatenate(total, axis=-1)


def per_device(activations, w_query, w_key, w_value, key_blocks, random_count, grad_out):
    seq_devices = lax.axis_size("seq")
    dp_devices = lax.axis_size("dp")
    position = lax.axis_index("seq")
    dp_index = lax.axis_index("dp")
    tokens = activations[0]
    grad_rows = grad_out[0]
    tok_count = tokens.shape[0]
    heads = w_query.shape[1] // HD
    kv_heads = w_key.shape[1] // HD
    query_cols = heads * HD
    kv_cols = kv_heads * HD
    all_cols = query_cols + 2 * kv_cols
    w_local = jnp.concatenate([w_query, w_key, w_value], axis=1)
    w_full = lax.all_gather(w_local, "seq", axis=0, tiled=True)
    projected = jnp.dot(tokens, w_full, preferred_element_type=jnp.float32).astype(jnp.bfloat16)
    queries = projected[:, :query_cols]
    key_proj = projected[:, query_cols : query_cols + kv_cols]
    value_proj = projected[:, query_cols + kv_cols :]
    query_pieces = queries.reshape(tok_count, heads, HD).transpose(1, 0, 2)
    grad_pieces = grad_rows.reshape(tok_count, heads, HD).transpose(1, 0, 2)
    paired = jnp.concatenate(
        [key_proj.reshape(tok_count, kv_heads, HD), value_proj.reshape(tok_count, kv_heads, HD)],
        axis=2,
    )
    kv_pieces = jnp.repeat(paired.transpose(1, 0, 2), GROUP, axis=0)
    sent = jnp.concatenate([query_pieces, grad_pieces, kv_pieces], axis=2)
    landed = lax.all_to_all(sent, "seq", split_axis=0, concat_axis=1, tiled=True)[0]
    head_q = landed[:, :HD]
    head_grad = landed[:, HD : 2 * HD]
    head_k = landed[:, 2 * HD : 3 * HD]
    head_v = landed[:, 3 * HD :]
    blocks_mine = lax.dynamic_index_in_dim(key_blocks, position, 0, keepdims=False)
    count_mine = lax.dynamic_index_in_dim(random_count, position, 0, keepdims=False)
    attended, grad_query, grad_kv = head_pass(
        head_q, head_k, head_v, head_grad, blocks_mine, count_mine
    )
    back_sent = jnp.concatenate(
        [
            attended.reshape(seq_devices, tok_count, HD),
            grad_query.reshape(seq_devices, tok_count, HD),
            grad_kv.astype(jnp.bfloat16).reshape(seq_devices, tok_count, 2 * HD),
        ],
        axis=2,
    )
    back = lax.all_to_all(back_sent, "seq", split_axis=0, concat_axis=0, tiled=True)
    back_out = back[:, :, :HD]
    back_query = back[:, :, HD : 2 * HD]
    back_kv = back[:, :, 2 * HD :]
    out_rows = back_out.transpose(1, 0, 2).reshape(tok_count, heads * HD)
    grad_q_rows = back_query.transpose(1, 0, 2).reshape(tok_count, heads * HD)
    kv_sum = jnp.sum(
        back_kv.reshape(kv_heads, GROUP, tok_count, 2 * HD), axis=1, dtype=jnp.float32
    ).astype(jnp.bfloat16)
    grad_k_rows = kv_sum[:, :, :HD].transpose(1, 0, 2).reshape(tok_count, kv_heads * HD)
    grad_v_rows = kv_sum[:, :, HD:].transpose(1, 0, 2).reshape(tok_count, kv_heads * HD)
    combined = jnp.concatenate([grad_q_rows, grad_k_rows, grad_v_rows], axis=1)
    contract = (((1,), (1,)), ((), ()))
    grad_x_rows = lax.dot_general(
        combined, w_full, contract, preferred_element_type=jnp.float32
    ).astype(jnp.bfloat16)
    factor = 1.0 / math.sqrt(tok_count * seq_devices * dp_devices)
    over_tokens = (((0,), (0,)), ((), ()))
    term = (
        lax.dot_general(tokens, combined, over_tokens, preferred_element_type=jnp.float32) * factor
    ).astype(jnp.bfloat16)
    half = all_cols // 2
    core = dp_index % 2
    pairs = [(i, i ^ 1) for i in range(dp_devices)]
    keep = lax.dynamic_slice_in_dim(term, core * half, half, axis=1)
    give = lax.dynamic_slice_in_dim(term, (1 - core) * half, half, axis=1)
    got = lax.ppermute(give, "dp", pairs)
    chip_sum = (keep.astype(jnp.float32) + got.astype(jnp.float32)).astype(jnp.bfloat16)
    rows = chip_sum.shape[0] // seq_devices
    by_z = chip_sum.reshape(seq_devices // RING_Z, RING_Z, rows, half).transpose(1, 0, 2, 3)
    by_y = ring_reduce_scatter(by_z, RING_Z, 1, position)
    part = ring_reduce_scatter(by_y, seq_devices // RING_Z, RING_Z, position)
    step = 2
    while step < dp_devices:
        mates = [(i, i ^ step) for i in range(dp_devices)]
        other = lax.ppermute(part, "dp", mates)
        part = (part.astype(jnp.float32) + other.astype(jnp.float32)).astype(jnp.bfloat16)
        step *= 2
    other_half = lax.ppermute(part, "dp", pairs)
    first = jnp.where(core == 0, part, other_half)
    second = jnp.where(core == 0, other_half, part)
    grad_all = jnp.concatenate([first, second], axis=1)
    grad_wq = grad_all[:, :query_cols]
    grad_wk = grad_all[:, query_cols : query_cols + kv_cols]
    grad_wv = grad_all[:, query_cols + kv_cols :]
    return (out_rows[None], grad_x_rows[None], grad_wq, grad_wk, grad_wv)


def solution(mesh):
    placed = (
        P("dp", "seq", None),
        P("seq", None),
        P("seq", None),
        P("seq", None),
        P(),
        P(),
        P("dp", "seq", None),
    )
    return jax.shard_map(
        per_device,
        mesh=mesh,
        in_specs=placed,
        out_specs=(
            P("dp", "seq", None),
            P("dp", "seq", None),
            P("seq", None),
            P("seq", None),
            P("seq", None),
        ),
        check_vma=False,
    )
```

profile of v0, /device:TPU:1, one launch (start us, length us, event | category | flops | bytes accessed | tf_op | source)
XLA Modules:
  0.0 566.1 jit_solution(12210671963242412984)
XLA Ops:
  10.4 113.4 %all-gather.2.cloned.1.call-done = bf16[2048,2560]{1,0:T(8,128)(2,1)} async-done(((bf16[64,2560]{1,0:T(8,128)(2,1)}), bf16[2048,2560]{1,0:T(8,128)(2,1)}) %all-gather.2.cloned.1.call-update) | async-done | bytes 10485776 | tf_op jit(solution)/shard_map/all_gather | solution.py:103
  123.7 6.9 %fusion.13 = bf16[128,2560]{0,1:T(8,128)(2,1)S(1)} fusion(bf16[2048,2560]{1,0:T(8,128)(2,1)} %all-gather.2.cloned.1.call-done, bf16[1,128,2048]{2,1,0:T(8,128)(2,1)S(1)} %copy-done), kind=kOutput, calls=%fused_computation.27 | convolution fusion | flops 1342504960 | bytes 11665408 | tf_op jit(solution)/shard_map/dot_general | solution.py:104
  132.5 5.6 all-to-all-start
  140.7 46.1 %all-to-all-done = bf16[32,128,256]{1,2,0:T(8,128)(2,1)} async-done(((bf16[32,128,256]{1,2,0:T(8,128)(2,1)}), bf16[32,128,256]{1,2,0:T(8,128)(2,1)}, u32[]{:S(2)}, u32[]{:S(2)}) %all-to-all-start) | async-done | bytes 2097184 | tf_op jit(solution)/shard_map/all_to_all | solution.py:116
  198.8 6.2 %copy.122 = bf16[224,128,64]{1,0,2:T(8,128)(2,1)} copy(bf16[224,128,64]{1,2,0:T(8,128)(2,1)} %gather_fusion) | data formatting | bytes 7340032 | tf_op jit(solution)/shard_map/gather | solution.py:24
  205.0 7.8 %reshape.152 = bf16[32,896,64]{1,0,2:T(8,128)(2,1)} reshape(bf16[224,128,64]{1,0,2:T(8,128)(2,1)} %copy.122) | data formatting | bytes 7340032 | tf_op jit(solution)/shard_map/reshape | solution.py:24
  215.8 6.2 %copy.127 = bf16[224,128,64]{1,0,2:T(8,128)(2,1)} copy(bf16[224,128,64]{1,2,0:T(8,128)(2,1)} %gather_fusion.1) | data formatting | bytes 7340032 | tf_op jit(solution)/shard_map/gather | solution.py:25
  222.0 7.8 %reshape.154 = bf16[32,896,64]{1,0,2:T(8,128)(2,1)} reshape(bf16[224,128,64]{1,0,2:T(8,128)(2,1)} %copy.127) | data formatting | bytes 7340032 | tf_op jit(solution)/shard_map/reshape | solution.py:25
  229.8 10.8 %fusion.77 = (f32[32,128]{1,0:T(8,128)S(1)}, f32[32,128,896]{2,1,0:T(8,128)}) fusion(pred[896]{0:T(1024)(128)(4,1)S(1)} %broadcast_bitcast_fusion, bf16[32,128,64]{2,1,0:T(8,128)(2,1)S(1)} %bitcast.152, bf16[32,896,64]{1,0,2:T(8,128)(2,1)} %reshape.152), kind=kOutput, calls=%fused_computation.119 | convolution fusion | flops 484443008 | bytes 18891648 | tf_op jit(solution)/shard_map/sub | solution.py:31
  240.6 9.3 %fusion.31 = bf16[32,128,64]{1,2,0:T(8,128)(2,1)S(1)} fusion(bf16[32,896,64]{1,0,2:T(8,128)(2,1)} %reshape.154, f32[32,128,896]{2,1,0:T(8,128)} %get-tuple-element.49, f32[32,128]{1,0:T(8,128)S(1)} %get-tuple-element.48), kind=kOutput, calls=%fused_computation.42 | convolution fusion | flops 477364224 | bytes 18890752 | tf_op jit(solution)/shard_map/gqk,gke->gqe/dot_general | solution.py:34
  249.9 9.8 %fusion.9 = f32[32,896,64]{1,2,0:T(8,128)} fusion(bf16[32,128,64]{2,1,0:T(8,128)(2,1)S(1)} %bitcast.162, f32[32,128,896]{2,1,0:T(8,128)} %get-tuple-element.49, f32[32,128]{1,0:T(8,128)S(1)} %get-tuple-element.48), kind=kOutput, calls=%fused_computation.22 | convolution fusion | flops 477102080 | bytes 22560768 | tf_op jit(solution)/shard_map/gqk,gqe->gke/dot_general | solution.py:48
  259.7 11.0 %multiply_reduce_fusion = (f32[32,128]{1,0:T(8,128)S(1)}, f32[32,128,896]{2,1,0:T(8,128)}) fusion(f32[32,128,896]{2,1,0:T(8,128)} %get-tuple-element.49, f32[32,128]{1,0:T(8,128)S(1)} %get-tuple-element.48, bf16[32,128,64]{2,1,0:T(8,128)(2,1)S(1)} %bitcast.163, bf16[32,896,64]{1,0,2:T(8,128)(2,1)S(1)} %copy-done.7), kind=kOutput, calls=%fused_computation.9 | convolution fusion | flops 480768000 | bytes 33587200 | tf_op jit(solution)/shard_map/gqe,gke->gqk/dot_general | solution.py:37
  270.7 10.8 %multiply_convert_fusion.1 = bf16[32,128,896]{2,1,0:T(8,128)(2,1)S(1)} fusion(f32[32,128,896]{2,1,0:T(8,128)} %get-tuple-element.51, f32[32,128]{1,0:T(8,128)S(1)} %get-tuple-element.50, f32[32,128,896]{2,1,0:T(8,128)} %get-tuple-element.49, f32[32,128]{1,0:T(8,128)S(1)} %get-tuple-element.48), kind=kLoop, calls=%fused_computation.8 | loop fusion | flops 14680064 | bytes 36732928 | tf_op jit(solution)/shard_map/convert_element_type | solution.py:39
  290.8 10.5 %pad_maximum_fusion = f32[32,896,128]{1,2,0:T(8,128)} fusion(f32[32,896,64]{1,2,0:T(8,128)} %fusion.9, f32[32,896,64]{1,2,0:T(8,128)} %broadcast_multiply_fusion), kind=kLoop, calls=%fused_computation.7 | loop fusion | flops 3670016 | bytes 29360128 | tf_op jit(solution)/shard_map/concatenate | solution.py:49
  301.3 16.1 %copy.136 = f32[32,896,128]{2,1,0:T(8,128)} copy(f32[32,896,128]{1,2,0:T(8,128)} %pad_maximum_fusion) | data formatting | bytes 29360128 | tf_op jit(solution)/shard_map/concatenate | solution.py:49
  317.4 16.0 %reshape.156 = f32[224,16384]{1,0:T(8,128)} reshape(f32[32,896,128]{2,1,0:T(8,128)} %copy.136) | data formatting | bytes 29360128 | tf_op jit(solution)/shard_map/reshape | solution.py:49
  335.1 9.1 %fusion.22 = bf16[32,128,128]{2,0,1:T(8,128)(2,1)S(1)} fusion(s32[224]{0:T(256)S(1)} %eq.47, f32[224,16384]{1,0:T(8,128)} %reshape.156), kind=kOutput, calls=%fused_computation.39 | convolution fusion | flops 1409817600 | bytes 15729536 | tf_op jit(solution)/shard_map/dot_general | solution.py:56
  347.9 7.1 %all-to-all-start.1 = ((bf16[32,128,256]{2,1,0:T(8,128)(2,1)}), bf16[32,128,256]{2,1,0:T(8,128)(2,1)S(1)}, u32[]{:S(2)}, u32[]{:S(2)}) async-start(bf16[32,128,256]{2,1,0:T(8,128)(2,1)} %copy.140), calls=%async_computation.1 | async-start | bytes 4194304 | tf_op jit(solution)/shard_map/all_to_all | solution.py:134
  355.0 48.6 %all-to-all-done.1 = bf16[32,128,256]{2,1,0:T(8,128)(2,1)S(1)} async-done(((bf16[32,128,256]{2,1,0:T(8,128)(2,1)}), bf16[32,128,256]{2,1,0:T(8,128)(2,1)S(1)}, u32[]{:S(2)}, u32[]{:S(2)}) %all-to-all-start.1) | async-done | bytes 2097184 | tf_op jit(solution)/shard_map/all_to_all | solution.py:134
  420.3 8.6 %collective-permute-done = bf16[2048,1280]{1,0:T(8,128)(2,1)} collective-permute-done((bf16[2048,1280]{1,0:T(8,128)(2,1)}, bf16[2048,1280]{1,0:T(8,128)(2,1)}, u32[]{:S(2)}, u32[]{:S(2)}) %collective-permute-start) | collective-permute-done | bytes 5242912 | tf_op jit(solution)/shard_map/ppermute | solution.py:160
  428.9 5.4 fusion.5
  439.9 7.0 %collective-permute-done.11 = bf16[4,64,640]{2,1,0:T(8,128)(2,1)} collective-permute-done((bf16[4,64,640]{2,1,0:T(8,128)(2,1)}, bf16[4,64,640]{2,1,0:T(8,128)(2,1)}, u32[]{:S(2)}, u32[]{:S(2)}) %collective-permute-start.11) | collective-permute-done | bytes 327712 | tf_op jit(solution)/shard_map/ppermute | solution.py:83
  534.7 13.0 %collective-permute-start.23 = (bf16[64,1280]{1,0:T(8,128)(2,1)S(1)}, bf16[64,1280]{1,0:T(8,128)(2,1)S(1)}, u32[]{:S(2)}, u32[]{:S(2)}) collective-permute-start(bf16[64,1280]{1,0:T(8,128)(2,1)S(1)} %add_convert_fusion), channel_id=1, source_target_pairs={{0,32},{32,0},{64,96},{96,64},{128,160},{160,128},{192,224},{224,1... | collective-permute-start | bytes 491528 | tf_op jit(solution)/shard_map/ppermute | solution.py:172
  547.7 8.5 %fusion.21 = bf16[1,128,2048]{2,1,0:T(8,128)(2,1)} fusion(bf16[2048,2560]{1,0:T(8,128)(2,1)} %all-gather.2.cloned.1.call-done, bf16[128,256]{0,1:T(8,128)(2,1)S(1)} %bitcast.165, bf16[128,256]{0,1:T(8,128)(2,1)S(1)} %bitcast.167, bf16[128,2048]{0,1:T(8,128)(2,1)} %bitcast.155), kind=kOutput, calls=%fused_computation.36 | convolution fusion | flops 1344405504 | bytes 11665408 | tf_op jit(solution)/shard_map/dot_general | solution.py:147
  (140 shorter events, 148.9 us)
Async XLA Ops:
  7.2 116.6 %all-gather.2.cloned.1.call-start = ((), (), s32[]{:S(2)}) async-start(), calls=%async_computation.2 | async-start | bytes 10813440 | tf_op jit(solution)/shard_map/all_gather | solution.py:103
  132.5 54.2 %all-to-all-start = ((bf16[32,128,256]{1,2,0:T(8,128)(2,1)}), bf16[32,128,256]{1,2,0:T(8,128)(2,1)}, u32[]{:S(2)}, u32[]{:S(2)}) async-start(bf16[32,128,256]{1,2,0:T(8,128)(2,1)} %pad_maximum_fusion.1), calls=%async_computation | async-start | bytes 4194304 | tf_op jit(solution)/shard_map/all_to_all | solution.py:116
  347.9 55.8 %all-to-all-start.1 = ((bf16[32,128,256]{2,1,0:T(8,128)(2,1)}), bf16[32,128,256]{2,1,0:T(8,128)(2,1)S(1)}, u32[]{:S(2)}, u32[]{:S(2)}) async-start(bf16[32,128,256]{2,1,0:T(8,128)(2,1)} %copy.140), calls=%async_computation.1 | async-start | bytes 4194304 | tf_op jit(solution)/shard_map/all_to_all | solution.py:134
  417.8 11.1 %collective-permute-start = (bf16[2048,1280]{1,0:T(8,128)(2,1)}, bf16[2048,1280]{1,0:T(8,128)(2,1)}, u32[]{:S(2)}, u32[]{:S(2)}) collective-permute-start(bf16[2048,1280]{1,0:T(8,128)(2,1)} %dynamic-slice_bitcast_fusion), channel_id=1, source_target_pairs={{0,32},{32,0},{64,96},{96,64},{128,160},{160,128},{192,224},{224,1... | collective-permute-start | bytes 15728648 | tf_op jit(solution)/shard_map/ppermute | solution.py:160
  437.7 9.2 %collective-permute-start.11 = (bf16[4,64,640]{2,1,0:T(8,128)(2,1)}, bf16[4,64,640]{2,1,0:T(8,128)(2,1)}, u32[]{:S(2)}, u32[]{:S(2)}) collective-permute-start(bf16[4,64,640]{2,1,0:T(8,128)(2,1)} %dynamic-slice_bitcast_fusion.1), channel_id=1, source_target_pairs={{1,0},{2,1},{3,2},{4,3},{5,4},{6,5},{7,6},{0,7},{9,8},{10,9},{11,1... | collective-permute-start | bytes 983048 | tf_op jit(solution)/shard_map/ppermute | solution.py:83
  438.9 11.7 %collective-permute-start.1 = (bf16[4,64,640]{2,1,0:T(8,128)(2,1)}, bf16[4,64,640]{2,1,0:T(8,128)(2,1)}, u32[]{:S(2)}, u32[]{:S(2)}) collective-permute-start(bf16[4,64,640]{2,1,0:T(8,128)(2,1)} %dynamic-slice_bitcast_fusion.2), channel_id=1, source_target_pairs={{0,1},{1,2},{2,3},{3,4},{4,5},{5,6},{6,7},{7,0},{8,9},{9,10},{10,1... | collective-permute-start | bytes 983048 | tf_op jit(solution)/shard_map/ppermute | solution.py:83
  448.8 8.5 %collective-permute-start.12 = (bf16[4,64,640]{2,1,0:T(8,128)(2,1)}, bf16[4,64,640]{2,1,0:T(8,128)(2,1)}, u32[]{:S(2)}, u32[]{:S(2)}) collective-permute-start(bf16[4,64,640]{2,1,0:T(8,128)(2,1)} %fusion.46), channel_id=1, source_target_pairs={{1,0},{2,1},{3,2},{4,3},{5,4},{6,5},{7,6},{0,7},{9,8},{10,9},{11,1... | collective-permute-start | bytes 983048 | tf_op jit(solution)/shard_map/ppermute | solution.py:83
  452.5 9.6 %collective-permute-start.2 = (bf16[4,64,640]{2,1,0:T(8,128)(2,1)}, bf16[4,64,640]{2,1,0:T(8,128)(2,1)}, u32[]{:S(2)}, u32[]{:S(2)}) collective-permute-start(bf16[4,64,640]{2,1,0:T(8,128)(2,1)} %fusion.53), channel_id=1, source_target_pairs={{0,1},{1,2},{2,3},{3,4},{4,5},{5,6},{6,7},{7,0},{8,9},{9,10},{10,1... | collective-permute-start | bytes 983048 | tf_op jit(solution)/shard_map/ppermute | solution.py:83
  459.2 8.1 %collective-permute-start.13 = (bf16[4,64,640]{2,1,0:T(8,128)(2,1)}, bf16[4,64,640]{2,1,0:T(8,128)(2,1)}, u32[]{:S(2)}, u32[]{:S(2)}) collective-permute-start(bf16[4,64,640]{2,1,0:T(8,128)(2,1)} %fusion.45), channel_id=1, source_target_pairs={{1,0},{2,1},{3,2},{4,3},{5,4},{6,5},{7,6},{0,7},{9,8},{10,9},{11,1... | collective-permute-start | bytes 983048 | tf_op jit(solution)/shard_map/ppermute | solution.py:83
  463.9 8.7 %collective-permute-start.3 = (bf16[4,64,640]{2,1,0:T(8,128)(2,1)}, bf16[4,64,640]{2,1,0:T(8,128)(2,1)}, u32[]{:S(2)}, u32[]{:S(2)}) collective-permute-start(bf16[4,64,640]{2,1,0:T(8,128)(2,1)} %fusion.52), channel_id=1, source_target_pairs={{0,1},{1,2},{2,3},{3,4},{4,5},{5,6},{6,7},{7,0},{8,9},{9,10},{10,1... | collective-permute-start | bytes 983048 | tf_op jit(solution)/shard_map/ppermute | solution.py:83
  469.2 7.7 %collective-permute-start.14 = (bf16[4,64,640]{2,1,0:T(8,128)(2,1)}, bf16[4,64,640]{2,1,0:T(8,128)(2,1)}, u32[]{:S(2)}, u32[]{:S(2)}) collective-permute-start(bf16[4,64,640]{2,1,0:T(8,128)(2,1)} %fusion.44), channel_id=1, source_target_pairs={{1,0},{2,1},{3,2},{4,3},{5,4},{6,5},{7,6},{0,7},{9,8},{10,9},{11,1... | collective-permute-start | bytes 983048 | tf_op jit(solution)/shard_map/ppermute | solution.py:83
  474.4 7.5 %collective-permute-start.4 = (bf16[4,64,640]{2,1,0:T(8,128)(2,1)}, bf16[4,64,640]{2,1,0:T(8,128)(2,1)}, u32[]{:S(2)}, u32[]{:S(2)}) collective-permute-start(bf16[4,64,640]{2,1,0:T(8,128)(2,1)} %fusion.51), channel_id=1, source_target_pairs={{0,1},{1,2},{2,3},{3,4},{4,5},{5,6},{6,7},{7,0},{8,9},{9,10},{10,1... | collective-permute-start | bytes 983048 | tf_op jit(solution)/shard_map/ppermute | solution.py:83
  478.8 7.5 %collective-permute-start.15 = (bf16[4,64,640]{2,1,0:T(8,128)(2,1)}, bf16[4,64,640]{2,1,0:T(8,128)(2,1)}, u32[]{:S(2)}, u32[]{:S(2)}) collective-permute-start(bf16[4,64,640]{2,1,0:T(8,128)(2,1)} %fusion.43), channel_id=1, source_target_pairs={{1,0},{2,1},{3,2},{4,3},{5,4},{6,5},{7,6},{0,7},{9,8},{10,9},{11,1... | collective-permute-start | bytes 983048 | tf_op jit(solution)/shard_map/ppermute | solution.py:83
  483.7 7.5 %collective-permute-start.5 = (bf16[4,64,640]{2,1,0:T(8,128)(2,1)}, bf16[4,64,640]{2,1,0:T(8,128)(2,1)}, u32[]{:S(2)}, u32[]{:S(2)}) collective-permute-start(bf16[4,64,640]{2,1,0:T(8,128)(2,1)} %fusion.50), channel_id=1, source_target_pairs={{0,1},{1,2},{2,3},{3,4},{4,5},{5,6},{6,7},{7,0},{8,9},{9,10},{10,1... | collective-permute-start | bytes 983048 | tf_op jit(solution)/shard_map/ppermute | solution.py:83
  488.1 7.5 %collective-permute-start.16 = (bf16[4,64,640]{2,1,0:T(8,128)(2,1)}, bf16[4,64,640]{2,1,0:T(8,128)(2,1)}, u32[]{:S(2)}, u32[]{:S(2)}) collective-permute-start(bf16[4,64,640]{2,1,0:T(8,128)(2,1)} %fusion.42), channel_id=1, source_target_pairs={{1,0},{2,1},{3,2},{4,3},{5,4},{6,5},{7,6},{0,7},{9,8},{10,9},{11,1... | collective-permute-start | bytes 983048 | tf_op jit(solution)/shard_map/ppermute | solution.py:83
  493.0 7.5 %collective-permute-start.6 = (bf16[4,64,640]{2,1,0:T(8,128)(2,1)}, bf16[4,64,640]{2,1,0:T(8,128)(2,1)}, u32[]{:S(2)}, u32[]{:S(2)}) collective-permute-start(bf16[4,64,640]{2,1,0:T(8,128)(2,1)} %fusion.49), channel_id=1, source_target_pairs={{0,1},{1,2},{2,3},{3,4},{4,5},{5,6},{6,7},{7,0},{8,9},{9,10},{10,1... | collective-permute-start | bytes 983048 | tf_op jit(solution)/shard_map/ppermute | solution.py:83
  497.4 7.5 %collective-permute-start.17 = (bf16[4,64,640]{2,1,0:T(8,128)(2,1)}, bf16[4,64,640]{2,1,0:T(8,128)(2,1)}, u32[]{:S(2)}, u32[]{:S(2)}) collective-permute-start(bf16[4,64,640]{2,1,0:T(8,128)(2,1)} %fusion.41), channel_id=1, source_target_pairs={{1,0},{2,1},{3,2},{4,3},{5,4},{6,5},{7,6},{0,7},{9,8},{10,9},{11,1... | collective-permute-start | bytes 983048 | tf_op jit(solution)/shard_map/ppermute | solution.py:83
  501.6 8.4 %collective-permute-start.7 = (bf16[4,64,640]{2,1,0:T(8,128)(2,1)S(1)}, bf16[4,64,640]{2,1,0:T(8,128)(2,1)S(1)}, u32[]{:S(2)}, u32[]{:S(2)}) collective-permute-start(bf16[4,64,640]{2,1,0:T(8,128)(2,1)S(1)} %fusion.48), channel_id=1, source_target_pairs={{0,1},{1,2},{2,3},{3,4},{4,5},{5,6},{6,7},{7,0},{8,9},{9,10},{10,1... | collective-permute-start | bytes 983048 | tf_op jit(solution)/shard_map/ppermute | solution.py:83
  506.1 5.2 collective-permute-start.18
  510.1 4.9 collective-permute-start.8
  515.0 4.6 collective-permute-start.9
  519.6 4.6 collective-permute-start.10
  528.8 5.8 %collective-permute-start.22 = (bf16[64,1280]{1,0:T(8,128)(2,1)S(1)}, bf16[64,1280]{1,0:T(8,128)(2,1)S(1)}, u32[]{:S(2)}, u32[]{:S(2)}) collective-permute-start(bf16[64,1280]{1,0:T(8,128)(2,1)S(1)} %add_convert_fusion.1), channel_id=1, source_target_pairs={{0,128},{32,160},{64,192},{96,224},{128,0},{160,32},{192,64},{224,... | collective-permute-start | bytes 491528 | tf_op jit(solution)/shard_map/ppermute | solution.py:169
  534.7 22.9 %collective-permute-start.23 = (bf16[64,1280]{1,0:T(8,128)(2,1)S(1)}, bf16[64,1280]{1,0:T(8,128)(2,1)S(1)}, u32[]{:S(2)}, u32[]{:S(2)}) collective-permute-start(bf16[64,1280]{1,0:T(8,128)(2,1)S(1)} %add_convert_fusion), channel_id=1, source_target_pairs={{0,32},{32,0},{64,96},{96,64},{128,160},{160,128},{192,224},{224,1... | collective-permute-start | bytes 491528 | tf_op jit(solution)/shard_map/ppermute | solution.py:172
  (14 other events, 224.5 us)
Sparse Core Ops, SparseCore 0:
  11.2 112.5 all-gather.1
where the time goes:
time: 572 us; the launch traced here: 566 us
  waiting for transfers between devices  258 us (45%)
  local copies, waits for them, and re-layouts  99.6 us (17%)
  matrix products  77.2 us (13%)
  starting transfers between devices  60.2 us (11%)
  other arithmetic  55.6 us (10%)
  between operations  15.4 us (3%)
    all_gather x1, waiting for transfers between devices, per_device(): w_full = lax.all_gather(w_local, 'seq', axis=0, tiled=True)  113 us
    all_to_all x1, waiting for transfers between devices, per_device(): lax.all_to_all(back_sent, 'seq', split_axis=0, concat_axis=0, tiled=True)  48.6 us
    all_to_all x1, waiting for transfers between devices, per_device(): lax.all_to_all(sent, 'seq', split_axis=0, concat_axis=1, tiled=True)[0]  46.1 us
    ppermute x20, waiting for transfers between devices, ring_reduce_scatter(): got = lax.ppermute(buf, 'seq', perm)  35.1 us
    ppermute x20, starting transfers between devices, ring_reduce_scatter(): got = lax.ppermute(buf, 'seq', perm)  27.9 us
    convert_element_type x20, other arithmetic, ring_reduce_scatter(): (got.astype(jnp.float32) + chunk(k + 1).astype(jnp.float32)).astype(jnp.b...  22.7 us
    concatenate x1, local copies, waits for them, and re-layouts, head_pass(): jnp.concatenate([grad_keys, grad_values], axis=-1)  16.1 us
    reshape x1, local copies, waits for them, and re-layouts, head_pass(): jnp.concatenate([grad_keys, grad_values], axis=-1)  16 us
  transfers between devices with their start and end apart: 27, of which 18 were waited for; matrix products, arithmetic and copies ran while one was open for 6% of the time, Pallas kernels for 0%

commit v1 on v0

--- a/solution.py
+++ b/solution.py
@@ -113,7 +113,14 @@
     )
     kv_pieces = jnp.repeat(paired.transpose(1, 0, 2), GROUP, axis=0)
     sent = jnp.concatenate([query_pieces, grad_pieces, kv_pieces], axis=2)
-    landed = lax.all_to_all(sent, "seq", split_axis=0, concat_axis=1, tiled=True)[0]
+
+    def screen_lift(sample):
+        return jnp.concatenate(
+            lax.all_to_all(jnp.stack(jnp.split(sample, lax.axis_size("seq"), 0), 0), "seq", 0, 0),
+            axis=1,
+        )
+
+    landed = screen_lift(sent)[0]
     head_q = landed[:, :HD]
     head_grad = landed[:, HD : 2 * HD]
     head_k = landed[:, 2 * HD : 3 * HD]

time: 572 us -> 588 us (1.028)
  local copies, waits for them, and re-layouts: 99.6 us -> 117 us
    unnamed x26 -> x55, local copies, waits for them, and re-layouts: 8.56 us -> 28.1 us
  transfers between devices with their start and end apart: 27 -> 27, of which waited for: 18 -> 17; matrix products, arithmetic and copies ran while one was open for 6% -> 6% of each run, Pallas kernels for 0% -> 0%
where the time goes in v1:
time: 588 us; the launch traced here: 582 us
  waiting for transfers between devices  257 us (44%)
  local copies, waits for them, and re-layouts  117 us (20%)
  matrix products  77 us (13%)
  starting transfers between devices  59.6 us (10%)
  other arithmetic  55.1 us (9%)
  between operations  15.7 us (3%)
    all_gather x1, waiting for transfers between devices, per_device(): w_full = lax.all_gather(w_local, 'seq', axis=0, tiled=True)  113 us
    all_to_all x1, waiting for transfers between devices, per_device(): lax.all_to_all(back_sent, 'seq', split_axis=0, concat_axis=0, tiled=True)  48.6 us
    all_to_all x1, waiting for transfers between devices, screen_lift(): lax.all_to_all(jnp.stack(jnp.split(sample, lax.axis_size('seq'), 0), 0),...  46.1 us
    ppermute x20, waiting for transfers between devices, ring_reduce_scatter(): got = lax.ppermute(buf, 'seq', perm)  34.6 us
    unnamed x55, local copies, waits for them, and re-layouts  28.1 us
    ppermute x20, starting transfers between devices, ring_reduce_scatter(): got = lax.ppermute(buf, 'seq', perm)  27.4 us
    convert_element_type x20, other arithmetic, ring_reduce_scatter(): (got.astype(jnp.float32) + chunk(k + 1).astype(jnp.float32)).astype(jnp.b...  22.7 us
    concatenate x1, local copies, waits for them, and re-layouts, head_pass(): jnp.concatenate([grad_keys, grad_values], axis=-1)  16.1 us
  transfers between devices with their start and end apart: 27, of which 17 were waited for; matrix products, arithmetic and copies ran while one was open for 6% of the time, Pallas kernels for 0%

profile of v1, /device:TPU:1, one launch (start us, length us, event | category | flops | bytes accessed | tf_op | source)
XLA Modules:
  0.0 581.6 jit_solution(11878209013802282436)
XLA Ops:
  10.9 112.9 %all-gather.2.cloned.1.call-done = bf16[2048,2560]{1,0:T(8,128)(2,1)} async-done(((bf16[64,2560]{1,0:T(8,128)(2,1)}), bf16[2048,2560]{1,0:T(8,128)(2,1)}) %all-gather.2.cloned.1.call-update) | async-done | bytes 10485776 | tf_op jit(solution)/shard_map/all_gather | solution.py:103
  123.7 6.9 %fusion.13 = bf16[128,2560]{0,1:T(8,128)(2,1)S(1)} fusion(bf16[2048,2560]{1,0:T(8,128)(2,1)} %all-gather.2.cloned.1.call-done, bf16[1,128,2048]{2,1,0:T(8,128)(2,1)S(1)} %copy-done), kind=kOutput, calls=%fused_computation.27 | convolution fusion | flops 1342504960 | bytes 11665408 | tf_op jit(solution)/shard_map/dot_general | solution.py:104
  152.8 5.7 all-to-all-start
  160.9 46.1 %all-to-all-done = bf16[32,1,128,256]{3,2,1,0:T(8,128)(2,1)S(1)} async-done(((bf16[32,1,128,256]{3,2,1,0:T(8,128)(2,1)}), bf16[32,1,128,256]{3,2,1,0:T(8,128)(2,1)S(1)}, u32[]{:S(2)}, u32[]{:S(2)}) %all-to-all-start) | async-done | bytes 2097184 | tf_op jit(solution)/shard_map/all_to_all | solution.py:119
  214.3 6.2 %copy.131 = bf16[224,128,64]{1,0,2:T(8,128)(2,1)} copy(bf16[224,128,64]{1,2,0:T(8,128)(2,1)} %gather_fusion) | data formatting | bytes 7340032 | tf_op jit(solution)/shard_map/gather | solution.py:24
  220.5 7.8 %reshape.148 = bf16[32,896,64]{1,0,2:T(8,128)(2,1)} reshape(bf16[224,128,64]{1,0,2:T(8,128)(2,1)} %copy.131) | data formatting | bytes 7340032 | tf_op jit(solution)/shard_map/reshape | solution.py:24
  231.6 6.2 %copy.136 = bf16[224,128,64]{1,0,2:T(8,128)(2,1)} copy(bf16[224,128,64]{1,2,0:T(8,128)(2,1)} %gather_fusion.1) | data formatting | bytes 7340032 | tf_op jit(solution)/shard_map/gather | solution.py:25
  237.8 7.9 %reshape.150 = bf16[32,896,64]{1,0,2:T(8,128)(2,1)} reshape(bf16[224,128,64]{1,0,2:T(8,128)(2,1)} %copy.136) | data formatting | bytes 7340032 | tf_op jit(solution)/shard_map/reshape | solution.py:25
  245.7 10.8 %fusion.109 = (f32[32,128]{1,0:T(8,128)S(1)}, f32[32,128,896]{2,1,0:T(8,128)}) fusion(pred[896]{0:T(1024)(128)(4,1)S(1)} %broadcast_bitcast_fusion, bf16[32,128,64]{2,1,0:T(8,128)(2,1)S(1)} %bitcast.279, bf16[32,896,64]{1,0,2:T(8,128)(2,1)} %reshape.148), kind=kOutput, calls=%fused_computation.183 | convolution fusion | flops 484443008 | bytes 18891648 | tf_op jit(solution)/shard_map/sub | solution.py:31
  256.5 9.3 %fusion.31 = bf16[32,128,64]{1,2,0:T(8,128)(2,1)S(1)} fusion(bf16[32,896,64]{1,0,2:T(8,128)(2,1)} %reshape.150, f32[32,128,896]{2,1,0:T(8,128)} %get-tuple-element.44, f32[32,128]{1,0:T(8,128)S(1)} %get-tuple-element.43), kind=kOutput, calls=%fused_computation.42 | convolution fusion | flops 477364224 | bytes 18890752 | tf_op jit(solution)/shard_map/gqk,gke->gqe/dot_general | solution.py:34
  265.8 10.9 %multiply_reduce_fusion = (f32[32,128]{1,0:T(8,128)S(1)}, f32[32,128,896]{2,1,0:T(8,128)}) fusion(f32[32,128,896]{2,1,0:T(8,128)} %get-tuple-element.44, f32[32,128]{1,0:T(8,128)S(1)} %get-tuple-element.43, bf16[32,128,64]{2,1,0:T(8,128)(2,1)S(1)} %bitcast.290, bf16[32,896,64]{1,0,2:T(8,128)(2,1)} %reshape.150), kind=kOutput, calls=%fused_computation.9 | convolution fusion | flops 480768000 | bytes 33587200 | tf_op jit(solution)/shard_map/gqe,gke->gqk/dot_general | solution.py:37
  276.7 10.9 %multiply_convert_fusion.1 = bf16[32,128,896]{2,1,0:T(8,128)(2,1)S(1)} fusion(f32[32,128,896]{2,1,0:T(8,128)} %get-tuple-element.46, f32[32,128]{1,0:T(8,128)S(1)} %get-tuple-element.45, f32[32,128,896]{2,1,0:T(8,128)} %get-tuple-element.44, f32[32,128]{1,0:T(8,128)S(1)} %get-tuple-element.43), kind=kLoop, calls=%fused_computation.8 | loop fusion | flops 14680064 | bytes 36732928 | tf_op jit(solution)/shard_map/convert_element_type | solution.py:39
  295.3 9.6 %fusion.9 = f32[32,896,64]{1,2,0:T(8,128)} fusion(bf16[32,128,64]{2,1,0:T(8,128)(2,1)S(1)} %bitcast.291, f32[32,128,896]{2,1,0:T(8,128)} %get-tuple-element.44, f32[32,128]{1,0:T(8,128)S(1)} %get-tuple-element.43), kind=kOutput, calls=%fused_computation.22 | convolution fusion | flops 477102080 | bytes 22560768 | tf_op jit(solution)/shard_map/gqk,gqe->gke/dot_general | solution.py:48
  309.0 10.6 %pad_maximum_fusion = f32[32,896,128]{1,2,0:T(8,128)} fusion(f32[32,896,64]{1,2,0:T(8,128)} %fusion.9, f32[32,896,64]{1,2,0:T(8,128)} %broadcast_multiply_fusion), kind=kLoop, calls=%fused_computation.7 | loop fusion | flops 3670016 | bytes 29360128 | tf_op jit(solution)/shard_map/concatenate | solution.py:49
  319.5 16.1 %copy.145 = f32[32,896,128]{2,1,0:T(8,128)} copy(f32[32,896,128]{1,2,0:T(8,128)} %pad_maximum_fusion) | data formatting | bytes 29360128 | tf_op jit(solution)/shard_map/concatenate | solution.py:49
  335.6 16.0 %reshape.152 = f32[224,16384]{1,0:T(8,128)} reshape(f32[32,896,128]{2,1,0:T(8,128)} %copy.145) | data formatting | bytes 29360128 | tf_op jit(solution)/shard_map/reshape | solution.py:49
  351.6 9.1 %fusion.22 = bf16[32,128,128]{2,0,1:T(8,128)(2,1)S(1)} fusion(s32[224]{0:T(256)S(1)} %eq.47, f32[224,16384]{1,0:T(8,128)} %reshape.152), kind=kOutput, calls=%fused_computation.39 | convolution fusion | flops 1409817600 | bytes 15729536 | tf_op jit(solution)/shard_map/dot_general | solution.py:56
  364.4 7.1 %all-to-all-start.1 = ((bf16[32,128,256]{2,1,0:T(8,128)(2,1)}), bf16[32,128,256]{2,1,0:T(8,128)(2,1)S(1)}, u32[]{:S(2)}, u32[]{:S(2)}) async-start(bf16[32,128,256]{2,1,0:T(8,128)(2,1)} %copy.149), calls=%async_computation.1 | async-start | bytes 4194304 | tf_op jit(solution)/shard_map/all_to_all | solution.py:141
  371.5 48.6 %all-to-all-done.1 = bf16[32,128,256]{2,1,0:T(8,128)(2,1)S(1)} async-done(((bf16[32,128,256]{2,1,0:T(8,128)(2,1)}), bf16[32,128,256]{2,1,0:T(8,128)(2,1)S(1)}, u32[]{:S(2)}, u32[]{:S(2)}) %all-to-all-start.1) | async-done | bytes 2097184 | tf_op jit(solution)/shard_map/all_to_all | solution.py:141
  436.8 8.6 %collective-permute-done = bf16[2048,1280]{1,0:T(8,128)(2,1)} collective-permute-done((bf16[2048,1280]{1,0:T(8,128)(2,1)}, bf16[2048,1280]{1,0:T(8,128)(2,1)}, u32[]{:S(2)}, u32[]{:S(2)}) %collective-permute-start) | collective-permute-done | bytes 5242912 | tf_op jit(solution)/shard_map/ppermute | solution.py:167
  445.4 5.4 fusion.5
  457.6 7.0 %collective-permute-done.1 = bf16[4,64,640]{2,1,0:T(8,128)(2,1)} collective-permute-done((bf16[4,64,640]{2,1,0:T(8,128)(2,1)}, bf16[4,64,640]{2,1,0:T(8,128)(2,1)}, u32[]{:S(2)}, u32[]{:S(2)}) %collective-permute-start.1) | collective-permute-done | bytes 327712 | tf_op jit(solution)/shard_map/ppermute | solution.py:83
  550.2 12.9 %collective-permute-start.23 = (bf16[64,1280]{1,0:T(8,128)(2,1)S(1)}, bf16[64,1280]{1,0:T(8,128)(2,1)S(1)}, u32[]{:S(2)}, u32[]{:S(2)}) collective-permute-start(bf16[64,1280]{1,0:T(8,128)(2,1)S(1)} %add_convert_fusion), channel_id=1, source_target_pairs={{0,32},{32,0},{64,96},{96,64},{128,160},{160,128},{192,224},{224,1... | collective-permute-start | bytes 491528 | tf_op jit(solution)/shard_map/ppermute | solution.py:179
  563.0 8.5 %fusion.21 = bf16[1,128,2048]{2,1,0:T(8,128)(2,1)} fusion(bf16[2048,2560]{1,0:T(8,128)(2,1)} %all-gather.2.cloned.1.call-done, bf16[128,256]{0,1:T(8,128)(2,1)S(1)} %bitcast.295, bf16[128,256]{0,1:T(8,128)(2,1)S(1)} %bitcast.293, bf16[128,2048]{0,1:T(8,128)(2,1)} %bitcast.282), kind=kOutput, calls=%fused_computation.36 | convolution fusion | flops 1344405504 | bytes 11665408 | tf_op jit(solution)/shard_map/dot_general | solution.py:154
  (172 shorter events, 164.9 us)
Async XLA Ops:
  7.2 116.6 %all-gather.2.cloned.1.call-start = ((), (), s32[]{:S(2)}) async-start(), calls=%async_computation.2 | async-start | bytes 10813440 | tf_op jit(solution)/shard_map/all_gather | solution.py:103
  152.8 54.3 %all-to-all-start = ((bf16[32,1,128,256]{3,2,1,0:T(8,128)(2,1)}), bf16[32,1,128,256]{3,2,1,0:T(8,128)(2,1)S(1)}, u32[]{:S(2)}, u32[]{:S(2)}) async-start(bf16[32,1,128,256]{3,2,1,0:T(8,128)(2,1)} %fusion.62), calls=%async_computation | async-start | bytes 4194304 | tf_op jit(solution)/shard_map/all_to_all | solution.py:119
  364.4 55.8 %all-to-all-start.1 = ((bf16[32,128,256]{2,1,0:T(8,128)(2,1)}), bf16[32,128,256]{2,1,0:T(8,128)(2,1)S(1)}, u32[]{:S(2)}, u32[]{:S(2)}) async-start(bf16[32,128,256]{2,1,0:T(8,128)(2,1)} %copy.149), calls=%async_computation.1 | async-start | bytes 4194304 | tf_op jit(solution)/shard_map/all_to_all | solution.py:141
  434.3 11.1 %collective-permute-start = (bf16[2048,1280]{1,0:T(8,128)(2,1)}, bf16[2048,1280]{1,0:T(8,128)(2,1)}, u32[]{:S(2)}, u32[]{:S(2)}) collective-permute-start(bf16[2048,1280]{1,0:T(8,128)(2,1)} %dynamic-slice_bitcast_fusion), channel_id=1, source_target_pairs={{0,32},{32,0},{64,96},{96,64},{128,160},{160,128},{192,224},{224,1... | collective-permute-start | bytes 15728648 | tf_op jit(solution)/shard_map/ppermute | solution.py:167
  454.2 10.5 %collective-permute-start.1 = (bf16[4,64,640]{2,1,0:T(8,128)(2,1)}, bf16[4,64,640]{2,1,0:T(8,128)(2,1)}, u32[]{:S(2)}, u32[]{:S(2)}) collective-permute-start(bf16[4,64,640]{2,1,0:T(8,128)(2,1)} %dynamic-slice_bitcast_fusion.2), channel_id=1, source_target_pairs={{0,1},{1,2},{2,3},{3,4},{4,5},{5,6},{6,7},{7,0},{8,9},{9,10},{10,1... | collective-permute-start | bytes 983048 | tf_op jit(solution)/shard_map/ppermute | solution.py:83
  456.2 10.6 %collective-permute-start.11 = (bf16[4,64,640]{2,1,0:T(8,128)(2,1)}, bf16[4,64,640]{2,1,0:T(8,128)(2,1)}, u32[]{:S(2)}, u32[]{:S(2)}) collective-permute-start(bf16[4,64,640]{2,1,0:T(8,128)(2,1)} %dynamic-slice_bitcast_fusion.1), channel_id=1, source_target_pairs={{1,0},{2,1},{3,2},{4,3},{5,4},{6,5},{7,6},{0,7},{9,8},{10,9},{11,1... | collective-permute-start | bytes 983048 | tf_op jit(solution)/shard_map/ppermute | solution.py:83
  466.6 9.7 %collective-permute-start.2 = (bf16[4,64,640]{2,1,0:T(8,128)(2,1)}, bf16[4,64,640]{2,1,0:T(8,128)(2,1)}, u32[]{:S(2)}, u32[]{:S(2)}) collective-permute-start(bf16[4,64,640]{2,1,0:T(8,128)(2,1)} %fusion.53), channel_id=1, source_target_pairs={{0,1},{1,2},{2,3},{3,4},{4,5},{5,6},{6,7},{7,0},{8,9},{9,10},{10,1... | collective-permute-start | bytes 983048 | tf_op jit(solution)/shard_map/ppermute | solution.py:83
  468.6 9.6 %collective-permute-start.12 = (bf16[4,64,640]{2,1,0:T(8,128)(2,1)}, bf16[4,64,640]{2,1,0:T(8,128)(2,1)}, u32[]{:S(2)}, u32[]{:S(2)}) collective-permute-start(bf16[4,64,640]{2,1,0:T(8,128)(2,1)} %fusion.46), channel_id=1, source_target_pairs={{1,0},{2,1},{3,2},{4,3},{5,4},{6,5},{7,6},{0,7},{9,8},{10,9},{11,1... | collective-permute-start | bytes 983048 | tf_op jit(solution)/shard_map/ppermute | solution.py:83
  478.2 8.6 %collective-permute-start.3 = (bf16[4,64,640]{2,1,0:T(8,128)(2,1)}, bf16[4,64,640]{2,1,0:T(8,128)(2,1)}, u32[]{:S(2)}, u32[]{:S(2)}) collective-permute-start(bf16[4,64,640]{2,1,0:T(8,128)(2,1)} %fusion.52), channel_id=1, source_target_pairs={{0,1},{1,2},{2,3},{3,4},{4,5},{5,6},{6,7},{7,0},{8,9},{9,10},{10,1... | collective-permute-start | bytes 983048 | tf_op jit(solution)/shard_map/ppermute | solution.py:83
  479.9 8.7 %collective-permute-start.13 = (bf16[4,64,640]{2,1,0:T(8,128)(2,1)}, bf16[4,64,640]{2,1,0:T(8,128)(2,1)}, u32[]{:S(2)}, u32[]{:S(2)}) collective-permute-start(bf16[4,64,640]{2,1,0:T(8,128)(2,1)} %fusion.45), channel_id=1, source_target_pairs={{1,0},{2,1},{3,2},{4,3},{5,4},{6,5},{7,6},{0,7},{9,8},{10,9},{11,1... | collective-permute-start | bytes 983048 | tf_op jit(solution)/shard_map/ppermute | solution.py:83
  488.6 7.5 %collective-permute-start.4 = (bf16[4,64,640]{2,1,0:T(8,128)(2,1)}, bf16[4,64,640]{2,1,0:T(8,128)(2,1)}, u32[]{:S(2)}, u32[]{:S(2)}) collective-permute-start(bf16[4,64,640]{2,1,0:T(8,128)(2,1)} %fusion.51), channel_id=1, source_target_pairs={{0,1},{1,2},{2,3},{3,4},{4,5},{5,6},{6,7},{7,0},{8,9},{9,10},{10,1... | collective-permute-start | bytes 983048 | tf_op jit(solution)/shard_map/ppermute | solution.py:83
  490.4 7.6 %collective-permute-start.14 = (bf16[4,64,640]{2,1,0:T(8,128)(2,1)}, bf16[4,64,640]{2,1,0:T(8,128)(2,1)}, u32[]{:S(2)}, u32[]{:S(2)}) collective-permute-start(bf16[4,64,640]{2,1,0:T(8,128)(2,1)} %fusion.44), channel_id=1, source_target_pairs={{1,0},{2,1},{3,2},{4,3},{5,4},{6,5},{7,6},{0,7},{9,8},{10,9},{11,1... | collective-permute-start | bytes 983048 | tf_op jit(solution)/shard_map/ppermute | solution.py:83
  498.0 7.5 %collective-permute-start.5 = (bf16[4,64,640]{2,1,0:T(8,128)(2,1)}, bf16[4,64,640]{2,1,0:T(8,128)(2,1)}, u32[]{:S(2)}, u32[]{:S(2)}) collective-permute-start(bf16[4,64,640]{2,1,0:T(8,128)(2,1)} %fusion.50), channel_id=1, source_target_pairs={{0,1},{1,2},{2,3},{3,4},{4,5},{5,6},{6,7},{7,0},{8,9},{9,10},{10,1... | collective-permute-start | bytes 983048 | tf_op jit(solution)/shard_map/ppermute | solution.py:83
  499.8 7.6 %collective-permute-start.15 = (bf16[4,64,640]{2,1,0:T(8,128)(2,1)}, bf16[4,64,640]{2,1,0:T(8,128)(2,1)}, u32[]{:S(2)}, u32[]{:S(2)}) collective-permute-start(bf16[4,64,640]{2,1,0:T(8,128)(2,1)} %fusion.43), channel_id=1, source_target_pairs={{1,0},{2,1},{3,2},{4,3},{5,4},{6,5},{7,6},{0,7},{9,8},{10,9},{11,1... | collective-permute-start | bytes 983048 | tf_op jit(solution)/shard_map/ppermute | solution.py:83
  507.3 7.5 %collective-permute-start.6 = (bf16[4,64,640]{2,1,0:T(8,128)(2,1)}, bf16[4,64,640]{2,1,0:T(8,128)(2,1)}, u32[]{:S(2)}, u32[]{:S(2)}) collective-permute-start(bf16[4,64,640]{2,1,0:T(8,128)(2,1)} %fusion.49), channel_id=1, source_target_pairs={{0,1},{1,2},{2,3},{3,4},{4,5},{5,6},{6,7},{7,0},{8,9},{9,10},{10,1... | collective-permute-start | bytes 983048 | tf_op jit(solution)/shard_map/ppermute | solution.py:83
  509.1 7.6 %collective-permute-start.16 = (bf16[4,64,640]{2,1,0:T(8,128)(2,1)}, bf16[4,64,640]{2,1,0:T(8,128)(2,1)}, u32[]{:S(2)}, u32[]{:S(2)}) collective-permute-start(bf16[4,64,640]{2,1,0:T(8,128)(2,1)} %fusion.42), channel_id=1, source_target_pairs={{1,0},{2,1},{3,2},{4,3},{5,4},{6,5},{7,6},{0,7},{9,8},{10,9},{11,1... | collective-permute-start | bytes 983048 | tf_op jit(solution)/shard_map/ppermute | solution.py:83
  516.7 7.5 %collective-permute-start.7 = (bf16[4,64,640]{2,1,0:T(8,128)(2,1)}, bf16[4,64,640]{2,1,0:T(8,128)(2,1)}, u32[]{:S(2)}, u32[]{:S(2)}) collective-permute-start(bf16[4,64,640]{2,1,0:T(8,128)(2,1)} %fusion.48), channel_id=1, source_target_pairs={{0,1},{1,2},{2,3},{3,4},{4,5},{5,6},{6,7},{7,0},{8,9},{9,10},{10,1... | collective-permute-start | bytes 983048 | tf_op jit(solution)/shard_map/ppermute | solution.py:83
  517.7 7.9 %collective-permute-start.17 = (bf16[4,64,640]{2,1,0:T(8,128)(2,1)S(1)}, bf16[4,64,640]{2,1,0:T(8,128)(2,1)S(1)}, u32[]{:S(2)}, u32[]{:S(2)}) collective-permute-start(bf16[4,64,640]{2,1,0:T(8,128)(2,1)S(1)} %fusion.41), channel_id=1, source_target_pairs={{1,0},{2,1},{3,2},{4,3},{5,4},{6,5},{7,6},{0,7},{9,8},{10,9},{11,1... | collective-permute-start | bytes 983048 | tf_op jit(solution)/shard_map/ppermute | solution.py:83
  525.3 5.0 collective-permute-start.8
  525.7 4.9 collective-permute-start.18
  530.3 4.8 collective-permute-start.9
  535.2 4.6 collective-permute-start.10
  544.3 5.8 collective-permute-start.22
  550.2 22.8 %collective-permute-start.23 = (bf16[64,1280]{1,0:T(8,128)(2,1)S(1)}, bf16[64,1280]{1,0:T(8,128)(2,1)S(1)}, u32[]{:S(2)}, u32[]{:S(2)}) collective-permute-start(bf16[64,1280]{1,0:T(8,128)(2,1)S(1)} %add_convert_fusion), channel_id=1, source_target_pairs={{0,32},{32,0},{64,96},{96,64},{128,160},{160,128},{192,224},{224,1... | collective-permute-start | bytes 491528 | tf_op jit(solution)/shard_map/ppermute | solution.py:179
  (13 other events, 205.4 us)
Sparse Core Ops, SparseCore 0:
  11.2 112.5 all-gather.1
